TPU v7x, 32 devices: a whole 2x2x4 slice. The times are simulated.
32 devices in a mesh: parts: 2 (over x), rows: 2 (over core), cols: 8 (over z, y).
Axes of the slice: x: 2, y: 2, z: 4, core: 2. Of those that a mesh axis runs over, the one named last changes fastest.
Arguments:
- src_feat: float32 [32, 131072], P(None, ('parts', 'rows', 'cols')), parts along dimension 1, may hold values from -0.75 to 0.75
- tgt_feat: float32 [32, 16384], P(None, ('parts', 'cols')), parts along dimension 1, may hold values from -0.75 to 0.75
- tgt_pot: float32 [16384], P(('parts', 'cols')), parts along dimension 0, may hold values from -25 to 25
- log_src: float32 [131072], P(('parts', 'rows', 'cols')), parts along dimension 0, may hold values from -3 to 3
- log_tgt: float32 [16384], P(('parts', 'cols')), parts along dimension 0, may hold values from -3 to 3
- pairs: int32 [512, 24], P(('parts', 'rows', 'cols')), parts along dimension 0, may hold values from 0 to 31, as said below
- counts: int32 [512], P(('parts', 'rows', 'cols')), parts along dimension 0, may hold values from 1 to 24, as said below
Outputs:
- src_pot: float32 [131072], P(('parts', 'rows', 'cols')), parts along dimension 0
- new_tgt_pot: float32 [16384], P(('parts', 'cols')), parts along dimension 0
There are 2 independent parts, one for each index of `parts`. A program takes and returns all parts, laid end to end along the dimension named above; each array names one. Nothing has to cross between parts.
Inputs may be any that keep to these rules, and one draw needn't show every extreme that they name: `pairs`: each row names 24 different target blocks, and every target block is the first entry of some row. `counts`: row 0 uses all 24 entries and row 1 only one.
All inputs are finite; a program needn't handle non-finite values.
Results may differ from a plain program's by a relative error of at most 0.0003.
Values sent between devices are 32-bit elements; how exact they have to be, the bound alone decides.
No kernel may reach another device: no remote copies, remote signals or barrier semaphores. Data moves between devices by JAX's collectives and lax.ppermute only.
A program may use at most 128 MiB of HBM per device.

v0:
```python
import jax
import jax.numpy as jnp
from jax import lax
from jax.sharding import PartitionSpec as P

D = 32
BLK = 256
GROUP = 8
epsilon = 0.1
NEG = -1e30


def joined(array, axis, combine):
    everything = jax.tree.map(lambda part: lax.all_gather(part, axis), array)
    initial = jax.tree.map(lambda part: part[0], everything)

    def step(k, so_far):
        return combine(so_far, jax.tree.map(lambda part: part[k], everything))

    return lax.fori_loop(1, lax.axis_size(axis), step, initial)


def combine_parts(first, second):
    top = jnp.maximum(first[0], second[0])
    total = first[1] * jnp.exp(first[0] - top) + second[1] * jnp.exp(second[0] - top)
    return (top, total)


def on_device(src_feat, tgt_feat, tgt_pot, log_src, log_tgt, pairs, counts):
    own_targets = tgt_feat.shape[1]
    packed = jnp.concatenate([tgt_feat, tgt_pot[None, :], log_tgt[None, :]], axis=0)
    whole = lax.all_gather(packed, "cols", axis=1, tiled=True)
    feats = whole[:D]
    ynorm = jnp.sum(feats * feats, axis=0)
    tblocks = whole.shape[1] // BLK
    table = jnp.concatenate([whole, ynorm[None, :]], axis=0)
    blocks = jnp.transpose(table.reshape(D + 3, tblocks, BLK), (1, 0, 2))
    within = jnp.arange(GROUP, dtype=jnp.int32)
    block_numbers = jnp.arange(tblocks, dtype=jnp.int32)

    def row_step(carry, index):
        start = index * BLK
        xs = lax.dynamic_slice_in_dim(src_feat, start, BLK, 1)
        weights = lax.dynamic_slice_in_dim(log_src, start, BLK, 0)
        xnorm = jnp.sum(xs * xs, axis=0)
        row_ids = pairs[index]
        count = counts[index]
        ngroups = (count + GROUP - 1) // GROUP
        slabs = jnp.take(blocks, row_ids, axis=0)

        def take_group(step):
            ids = lax.dynamic_slice_in_dim(row_ids, step * GROUP, GROUP, 0)
            group = lax.dynamic_slice_in_dim(slabs, step * GROUP, GROUP, 0)
            mask = jnp.repeat(step * GROUP + within < count, BLK)
            cross = jnp.einsum(
                "dr,gdc->rgc",
                xs,
                group[:, :D, :],
                precision=lax.Precision.HIGHEST,
                preferred_element_type=jnp.float32,
            ).reshape(BLK, GROUP * BLK)
            cost = xnorm[:, None] + group[:, D + 2, :].reshape(-1)[None, :] - 2.0 * cross
            return (ids, mask, group, cost)

        def row_pass(step, state):
            run_top, run_sum = state
            ids, mask, group, cost = take_group(step)
            pots = group[:, D, :].reshape(-1)
            logs = group[:, D + 1, :].reshape(-1)
            scores = jnp.where(mask[None, :], logs[None, :] + (pots[None, :] - cost) / epsilon, NEG)
            top = jnp.maximum(run_top, jnp.max(scores, axis=1))
            run_sum = run_sum * jnp.exp(run_top - top) + jnp.sum(
                jnp.exp(scores - top[:, None]), axis=1
            )
            return (top, run_sum)

        start_state = (jnp.full((BLK,), NEG, jnp.float32), jnp.zeros((BLK,), jnp.float32))
        run_top, run_sum = lax.fori_loop(0, ngroups, row_pass, start_state)
        fpot = -epsilon * (run_top + jnp.log(run_sum))

        def col_pass(step, state):
            acc_top, acc_sum = state
            ids, mask, group, cost = take_group(step)
            scores = jnp.where(
                mask[None, :], weights[:, None] + (fpot[:, None] - cost) / epsilon, NEG
            )
            col_top = jnp.max(scores, axis=0)
            col_sum = jnp.where(mask, jnp.sum(jnp.exp(scores - col_top[None, :]), axis=0), 0.0)
            col_top = col_top.reshape(GROUP, BLK)
            col_sum = col_sum.reshape(GROUP, BLK)
            selector = ids[:, None] == block_numbers[None, :]
            onehot = selector.astype(jnp.float32)
            landed = jnp.max(jnp.where(selector[:, :, None], col_top[:, None, :], NEG), axis=0)
            top = jnp.maximum(acc_top, landed)
            top_here = jnp.einsum(
                "gt,tb->gb",
                onehot,
                top,
                precision=lax.Precision.HIGHEST,
                preferred_element_type=jnp.float32,
            )
            added = jnp.einsum(
                "gt,gb->tb",
                onehot,
                col_sum * jnp.exp(col_top - top_here),
                precision=lax.Precision.HIGHEST,
                preferred_element_type=jnp.float32,
            )
            fresh = acc_sum * jnp.exp(acc_top - top) + added
            return (top, fresh)

        carry = lax.fori_loop(0, ngroups, col_pass, carry)
        return (carry, fpot)

    init = (jnp.full((tblocks, BLK), NEG, jnp.float32), jnp.zeros((tblocks, BLK), jnp.float32))
    (acc_top, acc_sum), fblocks = lax.scan(
        row_step, init, jnp.arange(pairs.shape[0], dtype=jnp.int32)
    )
    src_pot = fblocks.reshape(-1)
    flat_top = acc_top.reshape(-1)
    flat_sum = acc_sum.reshape(-1)
    owner_start = lax.axis_index("cols") * own_targets
    all_top, all_sum = joined((flat_top, flat_sum), ("rows", "cols"), combine_parts)
    own_top = lax.dynamic_slice_in_dim(all_top, owner_start, own_targets, 0)
    own_sum = lax.dynamic_slice_in_dim(all_sum, owner_start, own_targets, 0)
    new_tgt_pot = -epsilon * (own_top + jnp.log(own_sum))
    return (src_pot, new_tgt_pot)


def solution(mesh):
    placed = (
        P(None, ("parts", "rows", "cols")),
        P(None, ("parts", "cols")),
        P(("parts", "cols")),
        P(("parts", "rows", "cols")),
        P(("parts", "cols")),
        P(("parts", "rows", "cols"), None),
        P(("parts", "rows", "cols")),
    )
    return jax.shard_map(
        on_device,
        mesh=mesh,
        in_specs=placed,
        out_specs=(P(("parts", "rows", "cols")), P(("parts", "cols"))),
        check_vma=False,
    )
```

profile of v0, /device:TPU:0, one launch (start us, length us, event | category | flops | bytes accessed | tf_op | source)
XLA Modules:
  0.0 660.8 jit_solution(5542897578245292571)
XLA Ops:
  8.9 46.1 %all-gather.4.cloned.1.call-done = f32[34,8192]{1,0:T(8,128)} async-done(((f32[34,1024]{1,0:T(8,128)}), f32[34,8192]{1,0:T(8,128)}) %all-gather.4.cloned.1.call-update) | async-done | bytes 1114128 | tf_op jit(solution)/shard_map/all_gather | solution.py:32
  57.9 446.4 %while.113 = (s32[]{:T(128)}, f32[32,256]{1,0:T(8,128)S(1)}, f32[32,256]{1,0:T(8,128)S(1)}, f32[16,256]{1,0:T(8,128)S(1)}, s32[16]{0:T(128)S(1)}, /*index=5*/s32...) while((s32[]{:T(128)}, f32[32,256]{1,0:T(8,128)S(1)}, ...), condition=%wide.region_12.13_spmd.clone.clone, body=%wide.region_1.12_spmd.clone.clone.sunk | while | flops 415103776 | bytes 13110493 | solution.py:116
  65.5 12.1 %while.114 = (s32[]{:T(128)}, f32[256]{0:T(256)S(1)}, f32[256]{0:T(256)S(1)}, s32[]{:T(128)}, s32[8]{0:T(128)S(1)}, /*index=5*/s32[]{:T(128)}, f32[24,35,256]{2,...) while((s32[]{:T(128)}, f32[256]{0:T(256)S(1)}, ...), condition=%wide.region_6.6_spmd, body=%wide.region_3.5_spmd.sunk | while | flops 206570016 | bytes 4627243 | solution.py:78
  66.3 2.9 fusion.43
  70.3 2.9 fusion.43
  74.4 2.9 fusion.43
  78.4 12.5 %while.115 = (s32[]{:T(128)}, f32[32,256]{1,0:T(8,128)S(1)}, f32[32,256]{1,0:T(8,128)S(1)}, s32[]{:T(128)}, s32[24]{0:T(128)S(1)}, /*index=5*/s32[32]{0:T(128)S(...) while((s32[]{:T(128)}, f32[32,256]{1,0:T(8,128)S(1)}, ...), condition=%wide.region_11.11_spmd, body=%wide.region_7.10_spmd.sunk | while | flops 208300816 | bytes 4961095 | solution.py:112
  98.5 4.1 while.114
  103.4 4.1 while.115
  115.1 12.1 %while.114 = (s32[]{:T(128)}, f32[256]{0:T(256)S(1)}, f32[256]{0:T(256)S(1)}, s32[]{:T(128)}, s32[8]{0:T(128)S(1)}, /*index=5*/s32[]{:T(128)}, f32[24,35,256]{2,...) while((s32[]{:T(128)}, f32[256]{0:T(256)S(1)}, ...), condition=%wide.region_6.6_spmd, body=%wide.region_3.5_spmd.sunk | while | flops 206570016 | bytes 4627243 | solution.py:78
  119.9 2.9 fusion.43
  124.0 2.9 fusion.43
  128.0 12.5 %while.115 = (s32[]{:T(128)}, f32[32,256]{1,0:T(8,128)S(1)}, f32[32,256]{1,0:T(8,128)S(1)}, s32[]{:T(128)}, s32[24]{0:T(128)S(1)}, /*index=5*/s32[32]{0:T(128)S(...) while((s32[]{:T(128)}, f32[32,256]{1,0:T(8,128)S(1)}, ...), condition=%wide.region_11.11_spmd, body=%wide.region_7.10_spmd.sunk | while | flops 208300816 | bytes 4961095 | solution.py:112
  148.1 8.1 %while.114 = (s32[]{:T(128)}, f32[256]{0:T(256)S(1)}, f32[256]{0:T(256)S(1)}, s32[]{:T(128)}, s32[8]{0:T(128)S(1)}, /*index=5*/s32[]{:T(128)}, f32[24,35,256]{2,...) while((s32[]{:T(128)}, f32[256]{0:T(256)S(1)}, ...), condition=%wide.region_6.6_spmd, body=%wide.region_3.5_spmd.sunk | while | flops 206570016 | bytes 4627243 | solution.py:78
  157.0 8.3 %while.115 = (s32[]{:T(128)}, f32[32,256]{1,0:T(8,128)S(1)}, f32[32,256]{1,0:T(8,128)S(1)}, s32[]{:T(128)}, s32[24]{0:T(128)S(1)}, /*index=5*/s32[32]{0:T(128)S(...) while((s32[]{:T(128)}, f32[32,256]{1,0:T(8,128)S(1)}, ...), condition=%wide.region_11.11_spmd, body=%wide.region_7.10_spmd.sunk | while | flops 208300816 | bytes 4961095 | solution.py:112
  173.0 12.1 %while.114 = (s32[]{:T(128)}, f32[256]{0:T(256)S(1)}, f32[256]{0:T(256)S(1)}, s32[]{:T(128)}, s32[8]{0:T(128)S(1)}, /*index=5*/s32[]{:T(128)}, f32[24,35,256]{2,...) while((s32[]{:T(128)}, f32[256]{0:T(256)S(1)}, ...), condition=%wide.region_6.6_spmd, body=%wide.region_3.5_spmd.sunk | while | flops 206570016 | bytes 4627243 | solution.py:78
  177.8 2.9 fusion.43
  185.9 12.5 %while.115 = (s32[]{:T(128)}, f32[32,256]{1,0:T(8,128)S(1)}, f32[32,256]{1,0:T(8,128)S(1)}, s32[]{:T(128)}, s32[24]{0:T(128)S(1)}, /*index=5*/s32[32]{0:T(128)S(...) while((s32[]{:T(128)}, f32[32,256]{1,0:T(8,128)S(1)}, ...), condition=%wide.region_11.11_spmd, body=%wide.region_7.10_spmd.sunk | while | flops 208300816 | bytes 4961095 | solution.py:112
  206.0 12.1 %while.114 = (s32[]{:T(128)}, f32[256]{0:T(256)S(1)}, f32[256]{0:T(256)S(1)}, s32[]{:T(128)}, s32[8]{0:T(128)S(1)}, /*index=5*/s32[]{:T(128)}, f32[24,35,256]{2,...) while((s32[]{:T(128)}, f32[256]{0:T(256)S(1)}, ...), condition=%wide.region_6.6_spmd, body=%wide.region_3.5_spmd.sunk | while | flops 206570016 | bytes 4627243 | solution.py:78
  218.9 12.5 %while.115 = (s32[]{:T(128)}, f32[32,256]{1,0:T(8,128)S(1)}, f32[32,256]{1,0:T(8,128)S(1)}, s32[]{:T(128)}, s32[24]{0:T(128)S(1)}, /*index=5*/s32[32]{0:T(128)S(...) while((s32[]{:T(128)}, f32[32,256]{1,0:T(8,128)S(1)}, ...), condition=%wide.region_11.11_spmd, body=%wide.region_7.10_spmd.sunk | while | flops 208300816 | bytes 4961095 | solution.py:112
  239.0 8.1 %while.114 = (s32[]{:T(128)}, f32[256]{0:T(256)S(1)}, f32[256]{0:T(256)S(1)}, s32[]{:T(128)}, s32[8]{0:T(128)S(1)}, /*index=5*/s32[]{:T(128)}, f32[24,35,256]{2,...) while((s32[]{:T(128)}, f32[256]{0:T(256)S(1)}, ...), condition=%wide.region_6.6_spmd, body=%wide.region_3.5_spmd.sunk | while | flops 206570016 | bytes 4627243 | solution.py:78
  247.9 8.3 %while.115 = (s32[]{:T(128)}, f32[32,256]{1,0:T(8,128)S(1)}, f32[32,256]{1,0:T(8,128)S(1)}, s32[]{:T(128)}, s32[24]{0:T(128)S(1)}, /*index=5*/s32[32]{0:T(128)S(...) while((s32[]{:T(128)}, f32[32,256]{1,0:T(8,128)S(1)}, ...), condition=%wide.region_11.11_spmd, body=%wide.region_7.10_spmd.sunk | while | flops 208300816 | bytes 4961095 | solution.py:112
  263.8 12.1 %while.114 = (s32[]{:T(128)}, f32[256]{0:T(256)S(1)}, f32[256]{0:T(256)S(1)}, s32[]{:T(128)}, s32[8]{0:T(128)S(1)}, /*index=5*/s32[]{:T(128)}, f32[24,35,256]{2,...) while((s32[]{:T(128)}, f32[256]{0:T(256)S(1)}, ...), condition=%wide.region_6.6_spmd, body=%wide.region_3.5_spmd.sunk | while | flops 206570016 | bytes 4627243 | solution.py:78
  268.7 2.9 fusion.43
  276.8 12.5 %while.115 = (s32[]{:T(128)}, f32[32,256]{1,0:T(8,128)S(1)}, f32[32,256]{1,0:T(8,128)S(1)}, s32[]{:T(128)}, s32[24]{0:T(128)S(1)}, /*index=5*/s32[32]{0:T(128)S(...) while((s32[]{:T(128)}, f32[32,256]{1,0:T(8,128)S(1)}, ...), condition=%wide.region_11.11_spmd, body=%wide.region_7.10_spmd.sunk | while | flops 208300816 | bytes 4961095 | solution.py:112
  296.9 8.1 %while.114 = (s32[]{:T(128)}, f32[256]{0:T(256)S(1)}, f32[256]{0:T(256)S(1)}, s32[]{:T(128)}, s32[8]{0:T(128)S(1)}, /*index=5*/s32[]{:T(128)}, f32[24,35,256]{2,...) while((s32[]{:T(128)}, f32[256]{0:T(256)S(1)}, ...), condition=%wide.region_6.6_spmd, body=%wide.region_3.5_spmd.sunk | while | flops 206570016 | bytes 4627243 | solution.py:78
  305.8 8.3 %while.115 = (s32[]{:T(128)}, f32[32,256]{1,0:T(8,128)S(1)}, f32[32,256]{1,0:T(8,128)S(1)}, s32[]{:T(128)}, s32[24]{0:T(128)S(1)}, /*index=5*/s32[32]{0:T(128)S(...) while((s32[]{:T(128)}, f32[32,256]{1,0:T(8,128)S(1)}, ...), condition=%wide.region_11.11_spmd, body=%wide.region_7.10_spmd.sunk | while | flops 208300816 | bytes 4961095 | solution.py:112
  321.7 8.1 %while.114 = (s32[]{:T(128)}, f32[256]{0:T(256)S(1)}, f32[256]{0:T(256)S(1)}, s32[]{:T(128)}, s32[8]{0:T(128)S(1)}, /*index=5*/s32[]{:T(128)}, f32[24,35,256]{2,...) while((s32[]{:T(128)}, f32[256]{0:T(256)S(1)}, ...), condition=%wide.region_6.6_spmd, body=%wide.region_3.5_spmd.sunk | while | flops 206570016 | bytes 4627243 | solution.py:78
  326.5 2.9 fusion.43
  330.6 8.3 %while.115 = (s32[]{:T(128)}, f32[32,256]{1,0:T(8,128)S(1)}, f32[32,256]{1,0:T(8,128)S(1)}, s32[]{:T(128)}, s32[24]{0:T(128)S(1)}, /*index=5*/s32[32]{0:T(128)S(...) while((s32[]{:T(128)}, f32[32,256]{1,0:T(8,128)S(1)}, ...), condition=%wide.region_11.11_spmd, body=%wide.region_7.10_spmd.sunk | while | flops 208300816 | bytes 4961095 | solution.py:112
  346.5 8.1 %while.114 = (s32[]{:T(128)}, f32[256]{0:T(256)S(1)}, f32[256]{0:T(256)S(1)}, s32[]{:T(128)}, s32[8]{0:T(128)S(1)}, /*index=5*/s32[]{:T(128)}, f32[24,35,256]{2,...) while((s32[]{:T(128)}, f32[256]{0:T(256)S(1)}, ...), condition=%wide.region_6.6_spmd, body=%wide.region_3.5_spmd.sunk | while | flops 206570016 | bytes 4627243 | solution.py:78
  351.3 2.9 fusion.43
  355.4 8.3 %while.115 = (s32[]{:T(128)}, f32[32,256]{1,0:T(8,128)S(1)}, f32[32,256]{1,0:T(8,128)S(1)}, s32[]{:T(128)}, s32[24]{0:T(128)S(1)}, /*index=5*/s32[32]{0:T(128)S(...) while((s32[]{:T(128)}, f32[32,256]{1,0:T(8,128)S(1)}, ...), condition=%wide.region_11.11_spmd, body=%wide.region_7.10_spmd.sunk | while | flops 208300816 | bytes 4961095 | solution.py:112
  371.3 8.1 %while.114 = (s32[]{:T(128)}, f32[256]{0:T(256)S(1)}, f32[256]{0:T(256)S(1)}, s32[]{:T(128)}, s32[8]{0:T(128)S(1)}, /*index=5*/s32[]{:T(128)}, f32[24,35,256]{2,...) while((s32[]{:T(128)}, f32[256]{0:T(256)S(1)}, ...), condition=%wide.region_6.6_spmd, body=%wide.region_3.5_spmd.sunk | while | flops 206570016 | bytes 4627243 | solution.py:78
  376.2 2.9 fusion.43
  380.2 8.3 %while.115 = (s32[]{:T(128)}, f32[32,256]{1,0:T(8,128)S(1)}, f32[32,256]{1,0:T(8,128)S(1)}, s32[]{:T(128)}, s32[24]{0:T(128)S(1)}, /*index=5*/s32[32]{0:T(128)S(...) while((s32[]{:T(128)}, f32[32,256]{1,0:T(8,128)S(1)}, ...), condition=%wide.region_11.11_spmd, body=%wide.region_7.10_spmd.sunk | while | flops 208300816 | bytes 4961095 | solution.py:112
  396.1 8.1 %while.114 = (s32[]{:T(128)}, f32[256]{0:T(256)S(1)}, f32[256]{0:T(256)S(1)}, s32[]{:T(128)}, s32[8]{0:T(128)S(1)}, /*index=5*/s32[]{:T(128)}, f32[24,35,256]{2,...) while((s32[]{:T(128)}, f32[256]{0:T(256)S(1)}, ...), condition=%wide.region_6.6_spmd, body=%wide.region_3.5_spmd.sunk | while | flops 206570016 | bytes 4627243 | solution.py:78
  401.0 2.9 fusion.43
  405.0 8.3 %while.115 = (s32[]{:T(128)}, f32[32,256]{1,0:T(8,128)S(1)}, f32[32,256]{1,0:T(8,128)S(1)}, s32[]{:T(128)}, s32[24]{0:T(128)S(1)}, /*index=5*/s32[32]{0:T(128)S(...) while((s32[]{:T(128)}, f32[32,256]{1,0:T(8,128)S(1)}, ...), condition=%wide.region_11.11_spmd, body=%wide.region_7.10_spmd.sunk | while | flops 208300816 | bytes 4961095 | solution.py:112
  421.0 12.1 %while.114 = (s32[]{:T(128)}, f32[256]{0:T(256)S(1)}, f32[256]{0:T(256)S(1)}, s32[]{:T(128)}, s32[8]{0:T(128)S(1)}, /*index=5*/s32[]{:T(128)}, f32[24,35,256]{2,...) while((s32[]{:T(128)}, f32[256]{0:T(256)S(1)}, ...), condition=%wide.region_6.6_spmd, body=%wide.region_3.5_spmd.sunk | while | flops 206570016 | bytes 4627243 | solution.py:78
  425.8 2.9 fusion.43
  433.9 12.5 %while.115 = (s32[]{:T(128)}, f32[32,256]{1,0:T(8,128)S(1)}, f32[32,256]{1,0:T(8,128)S(1)}, s32[]{:T(128)}, s32[24]{0:T(128)S(1)}, /*index=5*/s32[32]{0:T(128)S(...) while((s32[]{:T(128)}, f32[32,256]{1,0:T(8,128)S(1)}, ...), condition=%wide.region_11.11_spmd, body=%wide.region_7.10_spmd.sunk | while | flops 208300816 | bytes 4961095 | solution.py:112
  454.0 12.1 %while.114 = (s32[]{:T(128)}, f32[256]{0:T(256)S(1)}, f32[256]{0:T(256)S(1)}, s32[]{:T(128)}, s32[8]{0:T(128)S(1)}, /*index=5*/s32[]{:T(128)}, f32[24,35,256]{2,...) while((s32[]{:T(128)}, f32[256]{0:T(256)S(1)}, ...), condition=%wide.region_6.6_spmd, body=%wide.region_3.5_spmd.sunk | while | flops 206570016 | bytes 4627243 | solution.py:78
  466.9 12.5 %while.115 = (s32[]{:T(128)}, f32[32,256]{1,0:T(8,128)S(1)}, f32[32,256]{1,0:T(8,128)S(1)}, s32[]{:T(128)}, s32[24]{0:T(128)S(1)}, /*index=5*/s32[32]{0:T(128)S(...) while((s32[]{:T(128)}, f32[32,256]{1,0:T(8,128)S(1)}, ...), condition=%wide.region_11.11_spmd, body=%wide.region_7.10_spmd.sunk | while | flops 208300816 | bytes 4961095 | solution.py:112
  487.0 8.1 %while.114 = (s32[]{:T(128)}, f32[256]{0:T(256)S(1)}, f32[256]{0:T(256)S(1)}, s32[]{:T(128)}, s32[8]{0:T(128)S(1)}, /*index=5*/s32[]{:T(128)}, f32[24,35,256]{2,...) while((s32[]{:T(128)}, f32[256]{0:T(256)S(1)}, ...), condition=%wide.region_6.6_spmd, body=%wide.region_3.5_spmd.sunk | while | flops 206570016 | bytes 4627243 | solution.py:78
  495.9 8.3 %while.115 = (s32[]{:T(128)}, f32[32,256]{1,0:T(8,128)S(1)}, f32[32,256]{1,0:T(8,128)S(1)}, s32[]{:T(128)}, s32[24]{0:T(128)S(1)}, /*index=5*/s32[32]{0:T(128)S(...) while((s32[]{:T(128)}, f32[32,256]{1,0:T(8,128)S(1)}, ...), condition=%wide.region_11.11_spmd, body=%wide.region_7.10_spmd.sunk | while | flops 208300816 | bytes 4961095 | solution.py:112
  504.4 114.5 %all-gather.1 = f32[16,1,8192]{2,1,0:T(1,128)S(1)} all-gather(f32[1,1,8192]{2,1,0:T(1,128)S(1)} %reshape.237), channel_id=1, replica_groups=mesh['parts'=2,'rows'=2,'cols'=8] {'rows','cols'}, dimensions={0}, use_global_device_ids=true | all-gather | bytes 557056 | tf_op jit(solution)/shard_map/all_gather | solution.py:14
  619.2 31.4 %all-gather = f32[16,1,8192]{2,1,0:T(1,128)S(1)} all-gather(f32[1,1,8192]{2,1,0:T(1,128)S(1)} %reshape.235), channel_id=1, replica_groups=mesh['parts'=2,'rows'=2,'cols'=8] {'rows','cols'}, dimensions={0}, use_global_device_ids=true | all-gather | bytes 557056 | tf_op jit(solution)/shard_map/all_gather | solution.py:14
  (1082 shorter events, 362.5 us)
Async XLA Ops:
  7.2 47.8 %all-gather.4.cloned.1.call-start = ((), (), s32[]{:S(2)}) async-start(), calls=%async_computation | async-start | bytes 1474560 | tf_op jit(solution)/shard_map/all_gather | solution.py:32
  55.0 2.0 copy-start
  57.1 0.9 copy-start.1
Sparse Core Ops, SparseCore 0:
  10.2 44.7 all-gather.3
where the time goes:
time: 665 us; the launch traced here: 661 us
  matrix products  216 us (32%)
  blocking collectives  146 us (22%)
  other arithmetic  126 us (19%)
  loops' own time  59.5 us (9%)
  local copies, waits for them, and re-layouts  53.3 us (8%)
  waiting for transfers between devices  46.1 us (7%)
  between operations  14.2 us (2%)
    dot_general x76, matrix products, take_group(): jnp.einsum('dr,gdc->rgc', xs, group[:, :D, :], precision=lax.Precision.HI...  198 us
    all_gather x2, blocking collectives, joined(): everything = jax.tree.map(lambda part: lax.all_gather(part, axis), array)  146 us
    another operation x1, loops' own time, on_device(): lax.scan(row_step, init, jnp.arange(pairs.shape[0], dtype=jnp.int32))  53.5 us
    lt x76, other arithmetic, take_group(): mask = jnp.repeat(step * GROUP + within < count, BLK)  52.8 us
    all_gather x1, waiting for transfers between devices, on_device(): whole = lax.all_gather(packed, 'cols', axis=1, tiled=True)  46.1 us
    reduce_sum x38, other arithmetic, row_pass(): jnp.sum(jnp.exp(scores - top[:, None]), axis=1)  13.7 us
    select_n x32, other arithmetic, row_step(): slabs = jnp.take(blocks, row_ids, axis=0)  13.3 us
  transfers between devices with their start and end apart: 1, of which 1 were waited for; matrix products, arithmetic and copies ran while one was open for 0% of the time, Pallas kernels for 0%

commit v1 on v0

--- a/solution.py
+++ b/solution.py
@@ -29,7 +29,12 @@
 def on_device(src_feat, tgt_feat, tgt_pot, log_src, log_tgt, pairs, counts):
     own_targets = tgt_feat.shape[1]
     packed = jnp.concatenate([tgt_feat, tgt_pot[None, :], log_tgt[None, :]], axis=0)
-    whole = lax.all_gather(packed, "cols", axis=1, tiled=True)
+    ring = [packed]
+    for hop in range(7):
+        ring.append(lax.ppermute(ring[-1], "cols", [(dev, (dev + 1) % 8) for dev in range(8)]))
+    whole = jnp.roll(
+        jnp.concatenate(ring[::-1], axis=1), (lax.axis_index("cols") + 1) * ring[0].shape[1], axis=1
+    )
     feats = whole[:D]
     ynorm = jnp.sum(feats * feats, axis=0)
     tblocks = whole.shape[1] // BLK

time: 665 us -> 653 us (0.982)
  between operations: 14.2 us -> 0.95 us
  waiting for transfers between devices: 46.1 us -> 56.6 us
  blocking collectives: 146 us -> 138 us
    ppermute x0 -> x7, waiting for transfers between devices: none -> 56.6 us  [on_device(): lax.ppermute(ring[-1], 'cols', [(dev, (dev + 1) % 8) for dev in range(8)])]
    all_gather x1 -> x0, waiting for transfers between devices: 46.1 us -> none  [on_device(): whole = lax.all_gather(packed, 'cols', axis=1, tiled=True)]
    all_gather x2, blocking collectives: 146 us -> 138 us  [joined(): everything = jax.tree.map(lambda part: lax.all_gather(part, axis), array)]
  transfers between devices with their start and end apart: 1 -> 7, of which waited for: 1 -> 7; matrix products, arithmetic and copies ran while one was open for 0% -> 0% of each run, Pallas kernels for 0% -> 0%
where the time goes in v1:
time: 653 us; the launch traced here: 645 us
  matrix products  216 us (33%)
  blocking collectives  138 us (21%)
  other arithmetic  121 us (19%)
  loops' own time  57.5 us (9%)
  waiting for transfers between devices  56.6 us (9%)
  local copies, waits for them, and re-layouts  51.6 us (8%)
    dot_general x76, matrix products, take_group(): jnp.einsum('dr,gdc->rgc', xs, group[:, :D, :], precision=lax.Precision.HI...  198 us
    all_gather x2, blocking collectives, joined(): everything = jax.tree.map(lambda part: lax.all_gather(part, axis), array)  138 us
    ppermute x7, waiting for transfers between devices, on_device(): lax.ppermute(ring[-1], 'cols', [(dev, (dev + 1) % 8) for dev in range(8)])  56.6 us
    another operation x1, loops' own time, on_device(): lax.scan(row_step, init, jnp.arange(pairs.shape[0], dtype=jnp.int32))  51.6 us
    lt x76, other arithmetic, take_group(): mask = jnp.repeat(step * GROUP + within < count, BLK)  48.4 us
    reduce_sum x38, other arithmetic, row_pass(): jnp.sum(jnp.exp(scores - top[:, None]), axis=1)  13.7 us
    select_n x32, other arithmetic, row_step(): slabs = jnp.take(blocks, row_ids, axis=0)  13.3 us
  transfers between devices with their start and end apart: 7, of which 7 were waited for; matrix products, arithmetic and copies ran while one was open for 0% of the time, Pallas kernels for 0%

profile of v1, /device:TPU:0, one launch (start us, length us, event | category | flops | bytes accessed | tf_op | source)
XLA Modules:
  0.0 644.9 jit_solution(18219105996446906004)
XLA Ops:
  1.7 3.0 collective-permute-start
  4.7 7.2 %collective-permute-done = f32[34,1024]{1,0:T(8,128)S(1)} collective-permute-done((f32[34,1024]{1,0:T(8,128)S(1)}, f32[34,1024]{1,0:T(8,128)S(1)}, u32[]{:S(2)}, u32[]{:S(2)}) %collective-permute-start) | collective-permute-done | bytes 139296 | tf_op jit(solution)/shard_map/ppermute | solution.py:34
  11.9 8.1 %collective-permute-done.1 = f32[34,1024]{1,0:T(8,128)S(1)} collective-permute-done((f32[34,1024]{1,0:T(8,128)S(1)}, f32[34,1024]{1,0:T(8,128)S(1)}, u32[]{:S(2)}, u32[]{:S(2)}) %collective-permute-start.1) | collective-permute-done | bytes 139296 | tf_op jit(solution)/shard_map/ppermute | solution.py:34
  20.0 8.0 %collective-permute-done.2 = f32[34,1024]{1,0:T(8,128)S(1)} collective-permute-done((f32[34,1024]{1,0:T(8,128)S(1)}, f32[34,1024]{1,0:T(8,128)S(1)}, u32[]{:S(2)}, u32[]{:S(2)}) %collective-permute-start.2) | collective-permute-done | bytes 139296 | tf_op jit(solution)/shard_map/ppermute | solution.py:34
  28.0 8.0 %collective-permute-done.3 = f32[34,1024]{1,0:T(8,128)S(1)} collective-permute-done((f32[34,1024]{1,0:T(8,128)S(1)}, f32[34,1024]{1,0:T(8,128)S(1)}, u32[]{:S(2)}, u32[]{:S(2)}) %collective-permute-start.3) | collective-permute-done | bytes 139296 | tf_op jit(solution)/shard_map/ppermute | solution.py:34
  36.0 8.0 %collective-permute-done.4 = f32[34,1024]{1,0:T(8,128)S(1)} collective-permute-done((f32[34,1024]{1,0:T(8,128)S(1)}, f32[34,1024]{1,0:T(8,128)S(1)}, u32[]{:S(2)}, u32[]{:S(2)}) %collective-permute-start.4) | collective-permute-done | bytes 139296 | tf_op jit(solution)/shard_map/ppermute | solution.py:34
  44.1 9.2 %collective-permute-done.5 = f32[34,1024]{1,0:T(8,128)S(1)} collective-permute-done((f32[34,1024]{1,0:T(8,128)S(1)}, f32[34,1024]{1,0:T(8,128)S(1)}, u32[]{:S(2)}, u32[]{:S(2)}) %collective-permute-start.5) | collective-permute-done | bytes 139296 | tf_op jit(solution)/shard_map/ppermute | solution.py:34
  53.3 8.0 %collective-permute-done.6 = f32[34,1024]{1,0:T(8,128)S(1)} collective-permute-done((f32[34,1024]{1,0:T(8,128)S(1)}, f32[34,1024]{1,0:T(8,128)S(1)}, u32[]{:S(2)}, u32[]{:S(2)}) %collective-permute-start.6) | collective-permute-done | bytes 139296 | tf_op jit(solution)/shard_map/ppermute | solution.py:34
  63.3 439.5 %while.113 = (s32[]{:T(128)}, f32[32,256]{1,0:T(8,128)S(1)}, f32[32,256]{1,0:T(8,128)S(1)}, f32[16,256]{1,0:T(8,128)S(1)}, s32[16]{0:T(128)S(1)}, /*index=5*/s32...) while((s32[]{:T(128)}, f32[32,256]{1,0:T(8,128)S(1)}, ...), condition=%wide.region_12.13_spmd.clone.clone, body=%wide.region_1.12_spmd.clone.clone.sunk | while | flops 415103776 | bytes 13110493 | solution.py:121
  70.7 12.0 %while.114 = (s32[]{:T(128)}, f32[256]{0:T(256)S(1)}, f32[256]{0:T(256)S(1)}, s32[]{:T(128)}, s32[8]{0:T(128)S(1)}, /*index=5*/s32[]{:T(128)}, f32[24,35,256]{2,...) while((s32[]{:T(128)}, f32[256]{0:T(256)S(1)}, ...), condition=%wide.region_6.6_spmd, body=%wide.region_3.5_spmd.sunk | while | flops 206570016 | bytes 4627243 | solution.py:83
  83.4 12.3 %while.115 = (s32[]{:T(128)}, f32[32,256]{1,0:T(8,128)S(1)}, f32[32,256]{1,0:T(8,128)S(1)}, s32[]{:T(128)}, s32[24]{0:T(128)S(1)}, /*index=5*/s32[32]{0:T(128)S(...) while((s32[]{:T(128)}, f32[32,256]{1,0:T(8,128)S(1)}, ...), condition=%wide.region_11.11_spmd, body=%wide.region_7.10_spmd.sunk | while | flops 208300816 | bytes 4961095 | solution.py:117
  103.2 4.0 while.114
  108.0 4.1 while.115
  119.5 12.0 %while.114 = (s32[]{:T(128)}, f32[256]{0:T(256)S(1)}, f32[256]{0:T(256)S(1)}, s32[]{:T(128)}, s32[8]{0:T(128)S(1)}, /*index=5*/s32[]{:T(128)}, f32[24,35,256]{2,...) while((s32[]{:T(128)}, f32[256]{0:T(256)S(1)}, ...), condition=%wide.region_6.6_spmd, body=%wide.region_3.5_spmd.sunk | while | flops 206570016 | bytes 4627243 | solution.py:83
  128.2 2.9 fusion.43
  132.3 12.3 %while.115 = (s32[]{:T(128)}, f32[32,256]{1,0:T(8,128)S(1)}, f32[32,256]{1,0:T(8,128)S(1)}, s32[]{:T(128)}, s32[24]{0:T(128)S(1)}, /*index=5*/s32[32]{0:T(128)S(...) while((s32[]{:T(128)}, f32[32,256]{1,0:T(8,128)S(1)}, ...), condition=%wide.region_11.11_spmd, body=%wide.region_7.10_spmd.sunk | while | flops 208300816 | bytes 4961095 | solution.py:117
  152.1 8.0 %while.114 = (s32[]{:T(128)}, f32[256]{0:T(256)S(1)}, f32[256]{0:T(256)S(1)}, s32[]{:T(128)}, s32[8]{0:T(128)S(1)}, /*index=5*/s32[]{:T(128)}, f32[24,35,256]{2,...) while((s32[]{:T(128)}, f32[256]{0:T(256)S(1)}, ...), condition=%wide.region_6.6_spmd, body=%wide.region_3.5_spmd.sunk | while | flops 206570016 | bytes 4627243 | solution.py:83
  156.8 2.9 fusion.43
  160.9 8.2 %while.115 = (s32[]{:T(128)}, f32[32,256]{1,0:T(8,128)S(1)}, f32[32,256]{1,0:T(8,128)S(1)}, s32[]{:T(128)}, s32[24]{0:T(128)S(1)}, /*index=5*/s32[32]{0:T(128)S(...) while((s32[]{:T(128)}, f32[32,256]{1,0:T(8,128)S(1)}, ...), condition=%wide.region_11.11_spmd, body=%wide.region_7.10_spmd.sunk | while | flops 208300816 | bytes 4961095 | solution.py:117
  176.5 12.0 %while.114 = (s32[]{:T(128)}, f32[256]{0:T(256)S(1)}, f32[256]{0:T(256)S(1)}, s32[]{:T(128)}, s32[8]{0:T(128)S(1)}, /*index=5*/s32[]{:T(128)}, f32[24,35,256]{2,...) while((s32[]{:T(128)}, f32[256]{0:T(256)S(1)}, ...), condition=%wide.region_6.6_spmd, body=%wide.region_3.5_spmd.sunk | while | flops 206570016 | bytes 4627243 | solution.py:83
  181.2 2.9 fusion.43
  185.2 2.9 fusion.43
  189.3 12.3 %while.115 = (s32[]{:T(128)}, f32[32,256]{1,0:T(8,128)S(1)}, f32[32,256]{1,0:T(8,128)S(1)}, s32[]{:T(128)}, s32[24]{0:T(128)S(1)}, /*index=5*/s32[32]{0:T(128)S(...) while((s32[]{:T(128)}, f32[32,256]{1,0:T(8,128)S(1)}, ...), condition=%wide.region_11.11_spmd, body=%wide.region_7.10_spmd.sunk | while | flops 208300816 | bytes 4961095 | solution.py:117
  209.0 12.0 %while.114 = (s32[]{:T(128)}, f32[256]{0:T(256)S(1)}, f32[256]{0:T(256)S(1)}, s32[]{:T(128)}, s32[8]{0:T(128)S(1)}, /*index=5*/s32[]{:T(128)}, f32[24,35,256]{2,...) while((s32[]{:T(128)}, f32[256]{0:T(256)S(1)}, ...), condition=%wide.region_6.6_spmd, body=%wide.region_3.5_spmd.sunk | while | flops 206570016 | bytes 4627243 | solution.py:83
  213.8 2.9 fusion.43
  221.8 12.3 %while.115 = (s32[]{:T(128)}, f32[32,256]{1,0:T(8,128)S(1)}, f32[32,256]{1,0:T(8,128)S(1)}, s32[]{:T(128)}, s32[24]{0:T(128)S(1)}, /*index=5*/s32[32]{0:T(128)S(...) while((s32[]{:T(128)}, f32[32,256]{1,0:T(8,128)S(1)}, ...), condition=%wide.region_11.11_spmd, body=%wide.region_7.10_spmd.sunk | while | flops 208300816 | bytes 4961095 | solution.py:117
  241.6 8.0 %while.114 = (s32[]{:T(128)}, f32[256]{0:T(256)S(1)}, f32[256]{0:T(256)S(1)}, s32[]{:T(128)}, s32[8]{0:T(128)S(1)}, /*index=5*/s32[]{:T(128)}, f32[24,35,256]{2,...) while((s32[]{:T(128)}, f32[256]{0:T(256)S(1)}, ...), condition=%wide.region_6.6_spmd, body=%wide.region_3.5_spmd.sunk | while | flops 206570016 | bytes 4627243 | solution.py:83
  250.4 8.2 %while.115 = (s32[]{:T(128)}, f32[32,256]{1,0:T(8,128)S(1)}, f32[32,256]{1,0:T(8,128)S(1)}, s32[]{:T(128)}, s32[24]{0:T(128)S(1)}, /*index=5*/s32[32]{0:T(128)S(...) while((s32[]{:T(128)}, f32[32,256]{1,0:T(8,128)S(1)}, ...), condition=%wide.region_11.11_spmd, body=%wide.region_7.10_spmd.sunk | while | flops 208300816 | bytes 4961095 | solution.py:117
  266.0 12.0 %while.114 = (s32[]{:T(128)}, f32[256]{0:T(256)S(1)}, f32[256]{0:T(256)S(1)}, s32[]{:T(128)}, s32[8]{0:T(128)S(1)}, /*index=5*/s32[]{:T(128)}, f32[24,35,256]{2,...) while((s32[]{:T(128)}, f32[256]{0:T(256)S(1)}, ...), condition=%wide.region_6.6_spmd, body=%wide.region_3.5_spmd.sunk | while | flops 206570016 | bytes 4627243 | solution.py:83
  278.8 12.3 %while.115 = (s32[]{:T(128)}, f32[32,256]{1,0:T(8,128)S(1)}, f32[32,256]{1,0:T(8,128)S(1)}, s32[]{:T(128)}, s32[24]{0:T(128)S(1)}, /*index=5*/s32[32]{0:T(128)S(...) while((s32[]{:T(128)}, f32[32,256]{1,0:T(8,128)S(1)}, ...), condition=%wide.region_11.11_spmd, body=%wide.region_7.10_spmd.sunk | while | flops 208300816 | bytes 4961095 | solution.py:117
  298.6 8.0 %while.114 = (s32[]{:T(128)}, f32[256]{0:T(256)S(1)}, f32[256]{0:T(256)S(1)}, s32[]{:T(128)}, s32[8]{0:T(128)S(1)}, /*index=5*/s32[]{:T(128)}, f32[24,35,256]{2,...) while((s32[]{:T(128)}, f32[256]{0:T(256)S(1)}, ...), condition=%wide.region_6.6_spmd, body=%wide.region_3.5_spmd.sunk | while | flops 206570016 | bytes 4627243 | solution.py:83
  307.3 8.2 %while.115 = (s32[]{:T(128)}, f32[32,256]{1,0:T(8,128)S(1)}, f32[32,256]{1,0:T(8,128)S(1)}, s32[]{:T(128)}, s32[24]{0:T(128)S(1)}, /*index=5*/s32[32]{0:T(128)S(...) while((s32[]{:T(128)}, f32[32,256]{1,0:T(8,128)S(1)}, ...), condition=%wide.region_11.11_spmd, body=%wide.region_7.10_spmd.sunk | while | flops 208300816 | bytes 4961095 | solution.py:117
  323.0 8.0 %while.114 = (s32[]{:T(128)}, f32[256]{0:T(256)S(1)}, f32[256]{0:T(256)S(1)}, s32[]{:T(128)}, s32[8]{0:T(128)S(1)}, /*index=5*/s32[]{:T(128)}, f32[24,35,256]{2,...) while((s32[]{:T(128)}, f32[256]{0:T(256)S(1)}, ...), condition=%wide.region_6.6_spmd, body=%wide.region_3.5_spmd.sunk | while | flops 206570016 | bytes 4627243 | solution.py:83
  331.8 8.2 %while.115 = (s32[]{:T(128)}, f32[32,256]{1,0:T(8,128)S(1)}, f32[32,256]{1,0:T(8,128)S(1)}, s32[]{:T(128)}, s32[24]{0:T(128)S(1)}, /*index=5*/s32[32]{0:T(128)S(...) while((s32[]{:T(128)}, f32[32,256]{1,0:T(8,128)S(1)}, ...), condition=%wide.region_11.11_spmd, body=%wide.region_7.10_spmd.sunk | while | flops 208300816 | bytes 4961095 | solution.py:117
  347.4 8.0 %while.114 = (s32[]{:T(128)}, f32[256]{0:T(256)S(1)}, f32[256]{0:T(256)S(1)}, s32[]{:T(128)}, s32[8]{0:T(128)S(1)}, /*index=5*/s32[]{:T(128)}, f32[24,35,256]{2,...) while((s32[]{:T(128)}, f32[256]{0:T(256)S(1)}, ...), condition=%wide.region_6.6_spmd, body=%wide.region_3.5_spmd.sunk | while | flops 206570016 | bytes 4627243 | solution.py:83
  356.2 8.2 %while.115 = (s32[]{:T(128)}, f32[32,256]{1,0:T(8,128)S(1)}, f32[32,256]{1,0:T(8,128)S(1)}, s32[]{:T(128)}, s32[24]{0:T(128)S(1)}, /*index=5*/s32[32]{0:T(128)S(...) while((s32[]{:T(128)}, f32[32,256]{1,0:T(8,128)S(1)}, ...), condition=%wide.region_11.11_spmd, body=%wide.region_7.10_spmd.sunk | while | flops 208300816 | bytes 4961095 | solution.py:117
  371.9 8.0 %while.114 = (s32[]{:T(128)}, f32[256]{0:T(256)S(1)}, f32[256]{0:T(256)S(1)}, s32[]{:T(128)}, s32[8]{0:T(128)S(1)}, /*index=5*/s32[]{:T(128)}, f32[24,35,256]{2,...) while((s32[]{:T(128)}, f32[256]{0:T(256)S(1)}, ...), condition=%wide.region_6.6_spmd, body=%wide.region_3.5_spmd.sunk | while | flops 206570016 | bytes 4627243 | solution.py:83
  380.6 8.2 %while.115 = (s32[]{:T(128)}, f32[32,256]{1,0:T(8,128)S(1)}, f32[32,256]{1,0:T(8,128)S(1)}, s32[]{:T(128)}, s32[24]{0:T(128)S(1)}, /*index=5*/s32[32]{0:T(128)S(...) while((s32[]{:T(128)}, f32[32,256]{1,0:T(8,128)S(1)}, ...), condition=%wide.region_11.11_spmd, body=%wide.region_7.10_spmd.sunk | while | flops 208300816 | bytes 4961095 | solution.py:117
  396.3 8.0 %while.114 = (s32[]{:T(128)}, f32[256]{0:T(256)S(1)}, f32[256]{0:T(256)S(1)}, s32[]{:T(128)}, s32[8]{0:T(128)S(1)}, /*index=5*/s32[]{:T(128)}, f32[24,35,256]{2,...) while((s32[]{:T(128)}, f32[256]{0:T(256)S(1)}, ...), condition=%wide.region_6.6_spmd, body=%wide.region_3.5_spmd.sunk | while | flops 206570016 | bytes 4627243 | solution.py:83
  405.1 8.2 %while.115 = (s32[]{:T(128)}, f32[32,256]{1,0:T(8,128)S(1)}, f32[32,256]{1,0:T(8,128)S(1)}, s32[]{:T(128)}, s32[24]{0:T(128)S(1)}, /*index=5*/s32[32]{0:T(128)S(...) while((s32[]{:T(128)}, f32[32,256]{1,0:T(8,128)S(1)}, ...), condition=%wide.region_11.11_spmd, body=%wide.region_7.10_spmd.sunk | while | flops 208300816 | bytes 4961095 | solution.py:117
  420.7 12.0 %while.114 = (s32[]{:T(128)}, f32[256]{0:T(256)S(1)}, f32[256]{0:T(256)S(1)}, s32[]{:T(128)}, s32[8]{0:T(128)S(1)}, /*index=5*/s32[]{:T(128)}, f32[24,35,256]{2,...) while((s32[]{:T(128)}, f32[256]{0:T(256)S(1)}, ...), condition=%wide.region_6.6_spmd, body=%wide.region_3.5_spmd.sunk | while | flops 206570016 | bytes 4627243 | solution.py:83
  433.5 12.3 %while.115 = (s32[]{:T(128)}, f32[32,256]{1,0:T(8,128)S(1)}, f32[32,256]{1,0:T(8,128)S(1)}, s32[]{:T(128)}, s32[24]{0:T(128)S(1)}, /*index=5*/s32[32]{0:T(128)S(...) while((s32[]{:T(128)}, f32[32,256]{1,0:T(8,128)S(1)}, ...), condition=%wide.region_11.11_spmd, body=%wide.region_7.10_spmd.sunk | while | flops 208300816 | bytes 4961095 | solution.py:117
  453.2 12.0 %while.114 = (s32[]{:T(128)}, f32[256]{0:T(256)S(1)}, f32[256]{0:T(256)S(1)}, s32[]{:T(128)}, s32[8]{0:T(128)S(1)}, /*index=5*/s32[]{:T(128)}, f32[24,35,256]{2,...) while((s32[]{:T(128)}, f32[256]{0:T(256)S(1)}, ...), condition=%wide.region_6.6_spmd, body=%wide.region_3.5_spmd.sunk | while | flops 206570016 | bytes 4627243 | solution.py:83
  466.0 12.3 %while.115 = (s32[]{:T(128)}, f32[32,256]{1,0:T(8,128)S(1)}, f32[32,256]{1,0:T(8,128)S(1)}, s32[]{:T(128)}, s32[24]{0:T(128)S(1)}, /*index=5*/s32[32]{0:T(128)S(...) while((s32[]{:T(128)}, f32[32,256]{1,0:T(8,128)S(1)}, ...), condition=%wide.region_11.11_spmd, body=%wide.region_7.10_spmd.sunk | while | flops 208300816 | bytes 4961095 | solution.py:117
  485.8 8.0 %while.114 = (s32[]{:T(128)}, f32[256]{0:T(256)S(1)}, f32[256]{0:T(256)S(1)}, s32[]{:T(128)}, s32[8]{0:T(128)S(1)}, /*index=5*/s32[]{:T(128)}, f32[24,35,256]{2,...) while((s32[]{:T(128)}, f32[256]{0:T(256)S(1)}, ...), condition=%wide.region_6.6_spmd, body=%wide.region_3.5_spmd.sunk | while | flops 206570016 | bytes 4627243 | solution.py:83
  494.6 8.2 %while.115 = (s32[]{:T(128)}, f32[32,256]{1,0:T(8,128)S(1)}, f32[32,256]{1,0:T(8,128)S(1)}, s32[]{:T(128)}, s32[24]{0:T(128)S(1)}, /*index=5*/s32[32]{0:T(128)S(...) while((s32[]{:T(128)}, f32[32,256]{1,0:T(8,128)S(1)}, ...), condition=%wide.region_11.11_spmd, body=%wide.region_7.10_spmd.sunk | while | flops 208300816 | bytes 4961095 | solution.py:117
  502.9 104.4 %all-gather.1 = f32[16,1,8192]{2,1,0:T(1,128)S(1)} all-gather(f32[1,1,8192]{2,1,0:T(1,128)S(1)} %reshape.237), channel_id=1, replica_groups=mesh['parts'=2,'rows'=2,'cols'=8] {'rows','cols'}, dimensions={0}, use_global_device_ids=true | all-gather | bytes 557056 | tf_op jit(solution)/shard_map/all_gather | solution.py:14
  607.6 33.9 %all-gather = f32[16,1,8192]{2,1,0:T(1,128)S(1)} all-gather(f32[1,1,8192]{2,1,0:T(1,128)S(1)} %reshape.235), channel_id=1, replica_groups=mesh['parts'=2,'rows'=2,'cols'=8] {'rows','cols'}, dimensions={0}, use_global_device_ids=true | all-gather | bytes 557056 | tf_op jit(solution)/shard_map/all_gather | solution.py:14
  (1114 shorter events, 376.0 us)
Async XLA Ops:
  0.6 60.8 %copy-start.2 = (f32[1024]{0:T(1024)S(1)}, f32[1024]{0:T(1024)}, u32[]{:S(2)}) copy-start(f32[1024]{0:T(1024)} %param.17) | copy-start | bytes 12292
  0.6 60.8 %copy-start.1 = (f32[1024]{0:T(1024)S(1)}, f32[1024]{0:T(1024)}, u32[]{:S(2)}) copy-start(f32[1024]{0:T(1024)} %param.19) | copy-start | bytes 12292
  0.7 60.8 %copy-start = (f32[32,1024]{1,0:T(8,128)S(1)}, f32[32,1024]{1,0:T(8,128)}, u32[]{:S(2)}) copy-start(f32[32,1024]{1,0:T(8,128)} %param.16) | copy-start | bytes 393220
  1.7 10.3 %collective-permute-start = (f32[34,1024]{1,0:T(8,128)S(1)}, f32[34,1024]{1,0:T(8,128)S(1)}, u32[]{:S(2)}, u32[]{:S(2)}) collective-permute-start(f32[34,1024]{1,0:T(8,128)S(1)} %pad_maximum_fusion), channel_id=1, source_target_pairs={{0,1},{1,2},{2,3},{3,4},{4,5},{5,6},{6,7},{7,0},{8,9},{9,10},{10,1... | collective-permute-start | bytes 417800 | tf_op jit(solution)/shard_map/ppermute | solution.py:34
  11.9 8.1 %collective-permute-start.1 = (f32[34,1024]{1,0:T(8,128)S(1)}, f32[34,1024]{1,0:T(8,128)S(1)}, u32[]{:S(2)}, u32[]{:S(2)}) collective-permute-start(f32[34,1024]{1,0:T(8,128)S(1)} %collective-permute-done), channel_id=1, source_target_pairs={{0,1},{1,2},{2,3},{3,4},{4,5},{5,6},{6,7},{7,0},{8,9},{9,10},{10,1... | collective-permute-start | bytes 417800 | tf_op jit(solution)/shard_map/ppermute | solution.py:34
  20.0 8.0 %collective-permute-start.2 = (f32[34,1024]{1,0:T(8,128)S(1)}, f32[34,1024]{1,0:T(8,128)S(1)}, u32[]{:S(2)}, u32[]{:S(2)}) collective-permute-start(f32[34,1024]{1,0:T(8,128)S(1)} %collective-permute-done.1), channel_id=1, source_target_pairs={{0,1},{1,2},{2,3},{3,4},{4,5},{5,6},{6,7},{7,0},{8,9},{9,10},{10,1... | collective-permute-start | bytes 417800 | tf_op jit(solution)/shard_map/ppermute | solution.py:34
  28.0 8.0 %collective-permute-start.3 = (f32[34,1024]{1,0:T(8,128)S(1)}, f32[34,1024]{1,0:T(8,128)S(1)}, u32[]{:S(2)}, u32[]{:S(2)}) collective-permute-start(f32[34,1024]{1,0:T(8,128)S(1)} %collective-permute-done.2), channel_id=1, source_target_pairs={{0,1},{1,2},{2,3},{3,4},{4,5},{5,6},{6,7},{7,0},{8,9},{9,10},{10,1... | collective-permute-start | bytes 417800 | tf_op jit(solution)/shard_map/ppermute | solution.py:34
  36.0 8.0 %collective-permute-start.4 = (f32[34,1024]{1,0:T(8,128)S(1)}, f32[34,1024]{1,0:T(8,128)S(1)}, u32[]{:S(2)}, u32[]{:S(2)}) collective-permute-start(f32[34,1024]{1,0:T(8,128)S(1)} %collective-permute-done.3), channel_id=1, source_target_pairs={{0,1},{1,2},{2,3},{3,4},{4,5},{5,6},{6,7},{7,0},{8,9},{9,10},{10,1... | collective-permute-start | bytes 417800 | tf_op jit(solution)/shard_map/ppermute | solution.py:34
  44.1 9.2 %collective-permute-start.5 = (f32[34,1024]{1,0:T(8,128)S(1)}, f32[34,1024]{1,0:T(8,128)S(1)}, u32[]{:S(2)}, u32[]{:S(2)}) collective-permute-start(f32[34,1024]{1,0:T(8,128)S(1)} %collective-permute-done.4), channel_id=1, source_target_pairs={{0,1},{1,2},{2,3},{3,4},{4,5},{5,6},{6,7},{7,0},{8,9},{9,10},{10,1... | collective-permute-start | bytes 417800 | tf_op jit(solution)/shard_map/ppermute | solution.py:34
  53.3 8.0 %collective-permute-start.6 = (f32[34,1024]{1,0:T(8,128)S(1)}, f32[34,1024]{1,0:T(8,128)S(1)}, u32[]{:S(2)}, u32[]{:S(2)}) collective-permute-start(f32[34,1024]{1,0:T(8,128)S(1)} %collective-permute-done.5), channel_id=1, source_target_pairs={{0,1},{1,2},{2,3},{3,4},{4,5},{5,6},{6,7},{7,0},{8,9},{9,10},{10,1... | collective-permute-start | bytes 417800 | tf_op jit(solution)/shard_map/ppermute | solution.py:34
  62.5 0.8 copy-start.3
